TPU v7x, 32 devices: a whole 2x2x4 slice. The times are simulated.
32 devices in a mesh: row: 8 (over y, x, core), col: 4 (over z).
Axes of the slice: x: 2, y: 2, z: 4, core: 2. Of those that a mesh axis runs over, the one named last changes fastest.
Arguments:
- features: bfloat16 [6144, 256], P(('col', 'row')), may hold values from -6 to 6
- edge_tiles: bfloat16 [8, 4, 12, 256, 256], P('row', 'col'), may hold values from 0.006225586 to 0.0625
- tile_rows: int32 [8, 4, 12], P('row', 'col'), may hold values from 0 to 2, as said below
- tile_cols: int32 [8, 4, 12], P('row', 'col'), may hold values from 0 to 5
- tile_count: int32 [8, 4], P('row', 'col'), may hold values from 3 to 12, as said below
- weight: bfloat16 [256, 256], replicated, may hold values from -0.375 to 0.375
- cotangent: bfloat16 [6144, 256], P(('row', 'col')), may hold values from -6 to 6
Outputs:
- activated: bfloat16 [6144, 256], P(('row', 'col'))
- feature_grad: bfloat16 [6144, 256], P(('col', 'row'))
Inputs may be any that keep to these rules, and one draw needn't show every extreme that they name: Within one device the pairs (tile_rows, tile_cols) of all 12 slots are distinct. Slots at or past tile_count hold no edges of the graph.
All inputs are finite; a program needn't handle non-finite values.
Results may differ from a plain program's by a relative error of at most 0.006.
Values may be sent and summed in bfloat16 or wider, within the bound.
No kernel may reach another device: no remote copies, remote signals or barrier semaphores. Data moves between devices by JAX's collectives and lax.ppermute only.
A program may use at most 64 MiB of HBM per device.

v0:
```python
import jax
import jax.numpy as jnp
from jax import lax
from jax.sharding import PartitionSpec as P


def silu_slope(mixed):
    sigma = jax.nn.sigmoid(mixed)
    return sigma * (1.0 + mixed * (1.0 - sigma))


def dense_layer(summed, grad_rows, weight):
    aggregated = summed.astype(jnp.bfloat16)
    mixed = jnp.dot(aggregated, weight, preferred_element_type=jnp.float32)
    activated = jax.nn.silu(mixed).astype(jnp.bfloat16)
    scaled = (grad_rows.astype(jnp.float32) * silu_slope(mixed)).astype(jnp.bfloat16)
    pulled = jnp.dot(scaled, weight.T, preferred_element_type=jnp.float32).astype(jnp.bfloat16)
    return (activated, pulled)


def place(results, targets, occupied, count):
    masked = results * occupied[:, None, None]
    return jax.ops.segment_sum(masked, targets, num_segments=count)


def on_device(features, edge_tiles, tile_rows, tile_cols, tile_count, weight, cotangent):
    blocks = edge_tiles[0, 0]
    row_slots = tile_rows[0, 0]
    col_slots = tile_cols[0, 0]
    filled = tile_count[0, 0]
    slot_total = blocks.shape[0]
    tile_size = blocks.shape[1]
    feat_width = features.shape[1]
    own_rows = features.shape[0]
    row_tiles = own_rows * lax.axis_size("col") // tile_size
    col_tiles = own_rows * lax.axis_size("row") // tile_size
    occupied = (jnp.arange(slot_total, dtype=jnp.int32) < filled).astype(jnp.float32)
    gathered = lax.all_gather(features, "row", axis=0, tiled=True)
    picked = gathered.reshape(col_tiles, tile_size, feat_width)[col_slots]
    products = jnp.einsum("kij,kjf->kif", blocks, picked, preferred_element_type=jnp.float32)
    partial_value = place(products, row_slots, occupied, row_tiles).reshape(
        row_tiles * tile_size, feat_width
    )
    own_sums = lax.psum_scatter(partial_value, "col", scatter_dimension=0, tiled=True)
    activated, pulled_own = dense_layer(own_sums, cotangent, weight)
    pulled_block = lax.all_gather(pulled_own, "col", axis=0, tiled=True)
    chosen = pulled_block.reshape(row_tiles, tile_size, feat_width)[row_slots]
    flipped = jnp.einsum("kij,kif->kjf", blocks, chosen, preferred_element_type=jnp.float32)
    partial_grad = place(flipped, col_slots, occupied, col_tiles).reshape(
        col_tiles * tile_size, feat_width
    )
    feature_grad = lax.psum_scatter(partial_grad, "row", scatter_dimension=0, tiled=True).astype(
        jnp.bfloat16
    )
    return (activated, feature_grad)


def solution(mesh):
    return jax.shard_map(
        on_device,
        mesh=mesh,
        in_specs=(
            P(("col", "row"), None),
            P("row", "col", None, None, None),
            P("row", "col", None),
            P("row", "col", None),
            P("row", "col"),
            P(),
            P(("row", "col"), None),
        ),
        out_specs=(P(("row", "col"), None), P(("col", "row"), None)),
        check_vma=False,
    )
```

profile of v0, /device:TPU:0, one launch (start us, length us, event | category | flops | bytes accessed | tf_op | source)
XLA Modules:
  0.0 138.2 jit_solution(2664074008607419204)
XLA Ops:
  7.2 0.0 reduce-scatter.3.cloned.1.call-start
  8.0 12.2 %all_gather.6 = bf16[1536,256]{1,0:T(8,128)(2,1)S(1)} all-gather(bf16[192,256]{1,0:T(8,128)(2,1)} %param.7), channel_id=1, replica_groups=mesh['row'=8,'col'=4] {'row'}, dimensions={0}, use_global_device_ids=true | all-gather | bytes 884736 | tf_op jit(solution)/shard_map/all_gather | solution.py:38
  20.2 0.7 fusion.4
  20.9 1.8 %gather_fusion = bf16[12,256,256]{2,1,0:T(8,128)(2,1)} fusion(bf16[6,256,256]{2,1,0:T(8,128)(2,1)S(1)} %bitcast.32, s32[1024]{0:T(1024)S(1)} %pad_clamp_fusion.1), kind=kCustom, calls=%fused_computation | custom fusion | bytes 3145776 | tf_op jit(solution)/shard_map/gather | solution.py:39
  22.7 3.8 %multiply_bitcast_fusion.1 = f32[12,256,256]{1,2,0:T(8,128)} fusion(bf16[12,256,256]{2,1,0:T(8,128)(2,1)} %gather_fusion, bf16[1,1,12,256,256]{4,3,2,1,0:T(8,128)(2,1)S(1)} %copy-done, f32[12]{0:T(128)S(1)} %compare_convert_fusion), kind=kOutput, calls=%fused_computation.5 | convolution fusion | flops 403439616 | bytes 6291504 | tf_op jit(solution)/shard_map/kij,kjf->kif/dot_general | solution.py:40
  26.6 3.6 %copy.12 = f32[12,256,256]{2,1,0:T(8,128)} copy(f32[12,256,256]{1,2,0:T(8,128)} %multiply_bitcast_fusion.1) | data formatting | bytes 6291456 | tf_op jit(solution)/shard_map/mul | solution.py:22
  30.1 0.1 broadcast_in_dim.4
  30.2 5.7 %scatter_fusion = f32[3,256,256]{2,1,0:T(8,128)S(1)} fusion(f32[3,256,256]{2,1,0:T(8,128)S(1)} %broadcast_in_dim.4, s32[12]{0:T(128)S(1)} %bitcast.33, f32[12,256,256]{2,1,0:T(8,128)} %copy.12), kind=kCustom, calls=%fused_computation.2 | custom fusion | flops 786432 | bytes 9437232 | tf_op jit(solution)/shard_map/scatter-add | solution.py:23
  36.0 0.9 copy-done.1
  36.8 0.0 reduce-scatter.3.cloned.1.call-update
  36.9 0.0 reduce-scatter.5.cloned.1.call-start
  36.9 23.5 %reduce-scatter.3.cloned.1.call-done = f32[192,256]{1,0:T(8,128)} async-done(((f32[768,256]{1,0:T(8,128)}), f32[192,256]{1,0:T(8,128)}) %reduce-scatter.3.cloned.1.call-update) | async-done | bytes 196624 | tf_op jit(solution)/shard_map/reduce_scatter | solution.py:44
  60.5 1.8 %multiply_convert_fusion.1 = (bf16[192,256]{1,0:T(8,128)(2,1)}, f32[192,256]{1,0:T(8,128)S(1)}) fusion(bf16[256,256]{1,0:T(8,128)(2,1)S(1)} %copy-done.5, f32[192,256]{1,0:T(8,128)} %reduce-scatter.3.cloned.1.call-done), kind=kOutput, calls=%fused_computation.10 | convolution fusion | flops 25460736 | bytes 622592 | tf_op jit(solution)/shard_map/dot_general | solution.py:14
  62.3 0.2 convolution_convert_fusion
  62.5 15.2 %all_gather.7 = bf16[768,256]{1,0:T(8,128)(2,1)S(1)} all-gather(bf16[192,256]{1,0:T(8,128)(2,1)S(1)} %convolution_convert_fusion), channel_id=1, replica_groups=mesh['row'=8,'col'=4] {'col'}, dimensions={0}, use_global_device_ids=true | all-gather | bytes 491520 | tf_op jit(solution)/shard_map/all_gather | solution.py:46
  77.7 0.6 gather_fusion.1
  78.4 2.4 %multiply_bitcast_fusion = f32[12,256,256]{1,2,0:T(8,128)} fusion(bf16[12,256,256]{2,1,0:T(8,128)(2,1)S(1)} %gather_fusion.1, bf16[1,1,12,256,256]{4,3,2,1,0:T(8,128)(2,1)S(1)} %copy-done, f32[12]{0:T(128)S(1)} %compare_convert_fusion), kind=kOutput, calls=%fused_computation.4 | convolution fusion | flops 403439616 | bytes 6291504 | tf_op jit(solution)/shard_map/kij,kif->kjf/dot_general | solution.py:48
  80.8 3.6 %copy.14 = f32[12,256,256]{2,1,0:T(8,128)} copy(f32[12,256,256]{1,2,0:T(8,128)} %multiply_bitcast_fusion) | data formatting | bytes 6291456 | tf_op jit(solution)/shard_map/mul | solution.py:22
  84.4 0.1 broadcast_in_dim.5
  84.5 0.5 copy-done.4
  85.0 5.8 %scatter_fusion.1 = f32[6,256,256]{2,1,0:T(8,128)S(1)} fusion(f32[6,256,256]{2,1,0:T(8,128)S(1)} %broadcast_in_dim.5, s32[12]{0:T(128)S(1)} %bitcast.34, f32[12,256,256]{2,1,0:T(8,128)} %copy.14), kind=kCustom, calls=%fused_computation.3 | custom fusion | flops 786432 | bytes 9437232 | tf_op jit(solution)/shard_map/scatter-add | solution.py:23
  90.8 1.2 copy-done.2
  92.0 37.8 %reduce-scatter.5.cloned.1.call-done = f32[192,256]{1,0:T(8,128)} async-done(((f32[1536,256]{1,0:T(8,128)}), f32[192,256]{1,0:T(8,128)}) %reduce-scatter.5.cloned.1.call-update) | async-done | bytes 196624 | tf_op jit(solution)/shard_map/reduce_scatter | solution.py:52
  129.8 1.6 %convert_element_type.31 = bf16[192,256]{1,0:T(8,128)(2,1)} convert(f32[192,256]{1,0:T(8,128)} %reduce-scatter.5.cloned.1.call-done) | non-fusion elementwise | flops 49152 | bytes 294912 | tf_op jit(solution)/shard_map/convert_element_type | solution.py:52
  (16 shorter events, 0.1 us)
Async XLA Ops:
  7.2 15.6 %copy-start = (bf16[1,1,12,256,256]{4,3,2,1,0:T(8,128)(2,1)S(1)}, bf16[1,1,12,256,256]{4,3,2,1,0:T(8,128)(2,1)}, u32[]{:S(2)}) copy-start(bf16[1,1,12,256,256]{4,3,2,1,0:T(8,128)(2,1)} %param.8) | copy-start | bytes 4718596
  7.2 53.3 %reduce-scatter.3.cloned.1.call-start = ((), (), s32[]{:S(2)}) async-start(), calls=%async_computation.2 | async-start | bytes 983040 | tf_op jit(solution)/shard_map/reduce_scatter | solution.py:44
  26.6 3.6 %copy-start.3 = (s32[1,1,12]{2,1,0:T(1,128)S(1)}, s32[1,1,12]{2,1,0:T(1,128)}, u32[]{:S(2)}) copy-start(s32[1,1,12]{2,1,0:T(1,128)} %param.9) | copy-start | bytes 148
  30.2 30.3 %copy-start.5 = (bf16[256,256]{1,0:T(8,128)(2,1)S(1)}, bf16[256,256]{1,0:T(8,128)(2,1)}, u32[]{:S(2)}) copy-start(bf16[256,256]{1,0:T(8,128)(2,1)} %param.12) | copy-start | bytes 393220
  36.0 0.9 copy-start.1
  36.0 26.3 %copy-start.6 = (bf16[192,256]{1,0:T(8,128)(2,1)S(1)}, bf16[192,256]{1,0:T(8,128)(2,1)}, u32[]{:S(2)}) copy-start(bf16[192,256]{1,0:T(8,128)(2,1)} %param.13) | copy-start | bytes 294916
  36.9 92.9 %reduce-scatter.5.cloned.1.call-start = ((), (), s32[]{:S(2)}) async-start(), calls=%async_computation.3 | async-start | bytes 1769472 | tf_op jit(solution)/shard_map/reduce_scatter | solution.py:52
  84.3 0.7 copy-start.4
  90.8 1.2 copy-start.2
Sparse Core Ops, SparseCore 0:
  37.0 23.4 reduce-scatter.2
  92.1 37.6 reduce-scatter.4
where the time goes:
time: 139 us; the launch traced here: 138 us
  waiting for transfers between devices  61.4 us (44%)
  blocking collectives  27.5 us (20%)
  between operations  14.9 us (11%)
  other arithmetic  13.7 us (10%)
  local copies, waits for them, and re-layouts  12.4 us (9%)
  matrix products  8.22 us (6%)
    reduce_scatter x1, waiting for transfers between devices, on_device(): lax.psum_scatter(partial_grad, 'row', scatter_dimension=0, tiled=True)  37.8 us
    reduce_scatter x1, waiting for transfers between devices, on_device(): lax.psum_scatter(partial_value, 'col', scatter_dimension=0, tiled=True)  23.5 us
    all_gather x1, blocking collectives, on_device(): pulled_block = lax.all_gather(pulled_own, 'col', axis=0, tiled=True)  15.2 us
    all_gather x1, blocking collectives, on_device(): gathered = lax.all_gather(features, 'row', axis=0, tiled=True)  12.2 us
    scatter-add x2, other arithmetic, place(): return jax.ops.segment_sum(masked, targets, num_segments=count)  11.5 us
    mul x2, local copies, waits for them, and re-layouts, place(): masked = results * occupied[:, None, None]  7.13 us
    dot_general x1, matrix products, on_device(): jnp.einsum('kij,kjf->kif', blocks, picked, preferred_element_type=jnp.flo...  3.81 us
  transfers between devices with their start and end apart: 2, of which 2 were waited for; matrix products, arithmetic and copies ran while one was open for 0% of the time, Pallas kernels for 0%

commit v1 on v0

--- a/solution.py
+++ b/solution.py
@@ -43,7 +43,16 @@
     )
     own_sums = lax.psum_scatter(partial_value, "col", scatter_dimension=0, tiled=True)
     activated, pulled_own = dense_layer(own_sums, cotangent, weight)
-    pulled_block = lax.all_gather(pulled_own, "col", axis=0, tiled=True)
+    ways = lax.axis_size("col")
+    up = [(d, (d + 1) % ways) for d in range(ways)]
+    down = [(d, (d - 1) % ways) for d in range(ways)]
+    earlier, later = ([pulled_own], [pulled_own])
+    for _ in range(ways // 2):
+        earlier.append(lax.ppermute(earlier[-1], "col", up))
+    for _ in range((ways - 1) // 2):
+        later.append(lax.ppermute(later[-1], "col", down))
+    line = jnp.concatenate([*earlier[::-1], *later[1:]], axis=0)
+    pulled_block = jnp.roll(line, (lax.axis_index("col") - ways // 2) * pulled_own.shape[0], axis=0)
     chosen = pulled_block.reshape(row_tiles, tile_size, feat_width)[row_slots]
     flipped = jnp.einsum("kij,kif->kjf", blocks, chosen, preferred_element_type=jnp.float32)
     partial_grad = place(flipped, col_slots, occupied, col_tiles).reshape(

time: 139 us -> 139 us (level)
  blocking collectives: 27.5 us -> 12.2 us
  waiting for transfers between devices: 61.4 us -> 72.4 us
  starting transfers between devices: 0.08 us -> 3.96 us
    all_gather x1 -> x0, blocking collectives: 15.2 us -> none  [on_device(): pulled_block = lax.all_gather(pulled_own, 'col', axis=0, tiled=True)]
    ppermute x0 -> x3, waiting for transfers between devices: none -> 8.98 us  [the longest x2 8.98 us: on_device(): earlier.append(lax.ppermute(earlier[-1], 'col', up))]
    ppermute x0 -> x3, starting transfers between devices: none -> 3.88 us  [the longest x1 3.82 us: on_device(): later.append(lax.ppermute(later[-1], 'col', down))]
    reduce_scatter x1, waiting for transfers between devices: 37.8 us -> 39.8 us  [on_device(): lax.psum_scatter(partial_grad, 'row', scatter_dimension=0, tiled=True)]
  transfers between devices with their start and end apart: 2 -> 5, of which waited for: 2 -> 4; matrix products, arithmetic and copies ran while one was open for 0% -> 0% of each run, Pallas kernels for 0% -> 0%
where the time goes in v1:
time: 139 us; the launch traced here: 138 us
  waiting for transfers between devices  72.4 us (52%)
  between operations  15 us (11%)
  other arithmetic  13.7 us (10%)
  local copies, waits for them, and re-layouts  12.5 us (9%)
  blocking collectives  12.2 us (9%)
  matrix products  8.24 us (6%)
  starting transfers between devices  3.96 us (3%)
    reduce_scatter x1, waiting for transfers between devices, on_device(): lax.psum_scatter(partial_grad, 'row', scatter_dimension=0, tiled=True)  39.8 us
    reduce_scatter x1, waiting for transfers between devices, on_device(): lax.psum_scatter(partial_value, 'col', scatter_dimension=0, tiled=True)  23.5 us
    all_gather x1, blocking collectives, on_device(): gathered = lax.all_gather(features, 'row', axis=0, tiled=True)  12.2 us
    scatter-add x2, other arithmetic, place(): return jax.ops.segment_sum(masked, targets, num_segments=count)  11.5 us
    ppermute x2, waiting for transfers between devices, on_device(): earlier.append(lax.ppermute(earlier[-1], 'col', up))  8.98 us
    mul x2, local copies, waits for them, and re-layouts, place(): masked = results * occupied[:, None, None]  7.11 us
    ppermute x1, starting transfers between devices, on_device(): later.append(lax.ppermute(later[-1], 'col', down))  3.82 us
    dot_general x1, matrix products, on_device(): jnp.einsum('kij,kjf->kif', blocks, picked, preferred_element_type=jnp.flo...  3.81 us
  transfers between devices with their start and end apart: 5, of which 4 were waited for; matrix products, arithmetic and copies ran while one was open for 0% of the time, Pallas kernels for 0%

profile of v1, /device:TPU:0, one launch (start us, length us, event | category | flops | bytes accessed | tf_op | source)
XLA Modules:
  0.0 138.1 jit_solution(15030874265350349775)
XLA Ops:
  8.0 12.2 %all_gather.3 = bf16[1536,256]{1,0:T(8,128)(2,1)S(1)} all-gather(bf16[192,256]{1,0:T(8,128)(2,1)} %param.7), channel_id=1, replica_groups=mesh['row'=8,'col'=4] {'row'}, dimensions={0}, use_global_device_ids=true | all-gather | bytes 884736 | tf_op jit(solution)/shard_map/all_gather | solution.py:38
  20.2 0.7 fusion.4
  20.9 1.9 %gather_fusion = bf16[12,256,256]{2,1,0:T(8,128)(2,1)} fusion(bf16[6,256,256]{2,1,0:T(8,128)(2,1)S(1)} %bitcast.32, s32[1024]{0:T(1024)S(1)} %pad_clamp_fusion.1), kind=kCustom, calls=%fused_computation | custom fusion | bytes 3145776 | tf_op jit(solution)/shard_map/gather | solution.py:39
  22.8 3.8 %multiply_bitcast_fusion.1 = f32[12,256,256]{1,2,0:T(8,128)} fusion(bf16[12,256,256]{2,1,0:T(8,128)(2,1)} %gather_fusion, bf16[1,1,12,256,256]{4,3,2,1,0:T(8,128)(2,1)S(1)} %copy-done, f32[12]{0:T(128)S(1)} %compare_convert_fusion), kind=kOutput, calls=%fused_computation.5 | convolution fusion | flops 403439616 | bytes 6291504 | tf_op jit(solution)/shard_map/kij,kjf->kif/dot_general | solution.py:40
  26.6 3.6 %copy.12 = f32[12,256,256]{2,1,0:T(8,128)} copy(f32[12,256,256]{1,2,0:T(8,128)} %multiply_bitcast_fusion.1) | data formatting | bytes 6291456 | tf_op jit(solution)/shard_map/mul | solution.py:22
  30.2 5.7 %scatter_fusion = f32[3,256,256]{2,1,0:T(8,128)S(1)} fusion(f32[3,256,256]{2,1,0:T(8,128)S(1)} %broadcast_in_dim.4, s32[12]{0:T(128)S(1)} %bitcast.33, f32[12,256,256]{2,1,0:T(8,128)} %copy.12), kind=kCustom, calls=%fused_computation.2 | custom fusion | flops 786432 | bytes 9437232 | tf_op jit(solution)/shard_map/scatter-add | solution.py:23
  36.0 0.9 copy-done.1
  36.9 23.5 %reduce-scatter.3.cloned.1.call-done = f32[192,256]{1,0:T(8,128)} async-done(((f32[768,256]{1,0:T(8,128)}), f32[192,256]{1,0:T(8,128)}) %reduce-scatter.3.cloned.1.call-update) | async-done | bytes 196624 | tf_op jit(solution)/shard_map/reduce_scatter | solution.py:44
  60.5 1.8 %multiply_convert_fusion.1 = (bf16[192,256]{1,0:T(8,128)(2,1)}, f32[192,256]{1,0:T(8,128)S(1)}) fusion(bf16[256,256]{1,0:T(8,128)(2,1)S(1)} %copy-done.5, f32[192,256]{1,0:T(8,128)} %reduce-scatter.3.cloned.1.call-done), kind=kOutput, calls=%fused_computation.10 | convolution fusion | flops 25460736 | bytes 622592 | tf_op jit(solution)/shard_map/dot_general | solution.py:14
  62.3 0.2 convolution_convert_fusion
  62.5 0.1 collective-permute-start
  62.6 6.4 %collective-permute-done = bf16[192,256]{1,0:T(8,128)(2,1)S(1)} collective-permute-done((bf16[192,256]{1,0:T(8,128)(2,1)S(1)}, bf16[192,256]{1,0:T(8,128)(2,1)S(1)}, u32[]{:S(2)}, u32[]{:S(2)}) %collective-permute-start) | collective-permute-done | bytes 98336 | tf_op jit(solution)/shard_map/ppermute | solution.py:51
  69.0 3.8 %collective-permute-start.2 = (bf16[192,256]{1,0:T(8,128)(2,1)S(1)}, bf16[192,256]{1,0:T(8,128)(2,1)S(1)}, u32[]{:S(2)}, u32[]{:S(2)}) collective-permute-start(bf16[192,256]{1,0:T(8,128)(2,1)S(1)} %convolution_convert_fusion), channel_id=1, source_target_pairs={{0,3},{1,0},{2,1},{3,2},{4,7},{5,4},{6,5},{7,6},{8,11},{9,8},{10,9... | collective-permute-start | bytes 294920 | tf_op jit(solution)/shard_map/ppermute | solution.py:53
  72.8 2.6 %collective-permute-done.1 = bf16[192,256]{1,0:T(8,128)(2,1)S(1)} collective-permute-done((bf16[192,256]{1,0:T(8,128)(2,1)S(1)}, bf16[192,256]{1,0:T(8,128)(2,1)S(1)}, u32[]{:S(2)}, u32[]{:S(2)}) %collective-permute-start.1) | collective-permute-done | bytes 98336 | tf_op jit(solution)/shard_map/ppermute | solution.py:51
  75.5 0.1 constant_dynamic-slice_fusion
  75.7 0.6 gather_fusion.1
  76.3 2.4 %multiply_bitcast_fusion = f32[12,256,256]{1,2,0:T(8,128)} fusion(bf16[12,256,256]{2,1,0:T(8,128)(2,1)S(1)} %gather_fusion.1, bf16[1,1,12,256,256]{4,3,2,1,0:T(8,128)(2,1)S(1)} %copy-done, f32[12]{0:T(128)S(1)} %compare_convert_fusion), kind=kOutput, calls=%fused_computation.4 | convolution fusion | flops 403439616 | bytes 6291504 | tf_op jit(solution)/shard_map/kij,kif->kjf/dot_general | solution.py:57
  78.7 3.6 %copy.14 = f32[12,256,256]{2,1,0:T(8,128)} copy(f32[12,256,256]{1,2,0:T(8,128)} %multiply_bitcast_fusion) | data formatting | bytes 6291456 | tf_op jit(solution)/shard_map/mul | solution.py:22
  82.3 0.1 broadcast_in_dim.5
  82.4 0.5 copy-done.4
  82.9 5.8 %scatter_fusion.1 = f32[6,256,256]{2,1,0:T(8,128)S(1)} fusion(f32[6,256,256]{2,1,0:T(8,128)S(1)} %broadcast_in_dim.5, s32[12]{0:T(128)S(1)} %bitcast.34, f32[12,256,256]{2,1,0:T(8,128)} %copy.14), kind=kCustom, calls=%fused_computation.3 | custom fusion | flops 786432 | bytes 9437232 | tf_op jit(solution)/shard_map/scatter-add | solution.py:23
  88.7 1.1 copy-done.2
  89.9 39.8 %reduce-scatter.5.cloned.1.call-done = f32[192,256]{1,0:T(8,128)} async-done(((f32[1536,256]{1,0:T(8,128)}), f32[192,256]{1,0:T(8,128)}) %reduce-scatter.5.cloned.1.call-update) | async-done | bytes 196624 | tf_op jit(solution)/shard_map/reduce_scatter | solution.py:61
  129.7 1.6 %convert_element_type.31 = bf16[192,256]{1,0:T(8,128)(2,1)} convert(f32[192,256]{1,0:T(8,128)} %reduce-scatter.5.cloned.1.call-done) | non-fusion elementwise | flops 49152 | bytes 294912 | tf_op jit(solution)/shard_map/convert_element_type | solution.py:61
  (30 shorter events, 0.3 us)
Async XLA Ops:
  7.2 15.6 %copy-start = (bf16[1,1,12,256,256]{4,3,2,1,0:T(8,128)(2,1)S(1)}, bf16[1,1,12,256,256]{4,3,2,1,0:T(8,128)(2,1)}, u32[]{:S(2)}) copy-start(bf16[1,1,12,256,256]{4,3,2,1,0:T(8,128)(2,1)} %param.8) | copy-start | bytes 4718596
  7.2 53.3 %reduce-scatter.3.cloned.1.call-start = ((), (), s32[]{:S(2)}) async-start(), calls=%async_computation.2 | async-start | bytes 983040 | tf_op jit(solution)/shard_map/reduce_scatter | solution.py:44
  26.6 3.6 %copy-start.3 = (s32[1,1,12]{2,1,0:T(1,128)S(1)}, s32[1,1,12]{2,1,0:T(1,128)}, u32[]{:S(2)}) copy-start(s32[1,1,12]{2,1,0:T(1,128)} %param.9) | copy-start | bytes 148
  30.2 30.3 %copy-start.5 = (bf16[256,256]{1,0:T(8,128)(2,1)S(1)}, bf16[256,256]{1,0:T(8,128)(2,1)}, u32[]{:S(2)}) copy-start(bf16[256,256]{1,0:T(8,128)(2,1)} %param.12) | copy-start | bytes 393220
  36.0 0.9 copy-start.1
  36.0 26.3 %copy-start.6 = (bf16[192,256]{1,0:T(8,128)(2,1)S(1)}, bf16[192,256]{1,0:T(8,128)(2,1)}, u32[]{:S(2)}) copy-start(bf16[192,256]{1,0:T(8,128)(2,1)} %param.13) | copy-start | bytes 294916
  36.9 92.8 %reduce-scatter.5.cloned.1.call-start = ((), (), s32[]{:S(2)}) async-start(), calls=%async_computation.3 | async-start | bytes 1769472 | tf_op jit(solution)/shard_map/reduce_scatter | solution.py:61
  62.5 6.5 %collective-permute-start = (bf16[192,256]{1,0:T(8,128)(2,1)S(1)}, bf16[192,256]{1,0:T(8,128)(2,1)S(1)}, u32[]{:S(2)}, u32[]{:S(2)}) collective-permute-start(bf16[192,256]{1,0:T(8,128)(2,1)S(1)} %convolution_convert_fusion), channel_id=1, source_target_pairs={{0,1},{1,2},{2,3},{3,0},{4,5},{5,6},{6,7},{7,4},{8,9},{9,10},{10,1... | collective-permute-start | bytes 294920 | tf_op jit(solution)/shard_map/ppermute | solution.py:51
  69.0 6.4 %collective-permute-start.1 = (bf16[192,256]{1,0:T(8,128)(2,1)S(1)}, bf16[192,256]{1,0:T(8,128)(2,1)S(1)}, u32[]{:S(2)}, u32[]{:S(2)}) collective-permute-start(bf16[192,256]{1,0:T(8,128)(2,1)S(1)} %collective-permute-done), channel_id=1, source_target_pairs={{0,1},{1,2},{2,3},{3,0},{4,5},{5,6},{6,7},{7,4},{8,9},{9,10},{10,1... | collective-permute-start | bytes 294920 | tf_op jit(solution)/shard_map/ppermute | solution.py:51
  69.0 6.5 %collective-permute-start.2 = (bf16[192,256]{1,0:T(8,128)(2,1)S(1)}, bf16[192,256]{1,0:T(8,128)(2,1)S(1)}, u32[]{:S(2)}, u32[]{:S(2)}) collective-permute-start(bf16[192,256]{1,0:T(8,128)(2,1)S(1)} %convolution_convert_fusion), channel_id=1, source_target_pairs={{0,3},{1,0},{2,1},{3,2},{4,7},{5,4},{6,5},{7,6},{8,11},{9,8},{10,9... | collective-permute-start | bytes 294920 | tf_op jit(solution)/shard_map/ppermute | solution.py:53
  82.3 0.7 copy-start.4
  88.7 1.2 copy-start.2
Sparse Core Ops, SparseCore 0:
  37.0 23.4 reduce-scatter.2
  90.0 39.6 reduce-scatter.4
